TPU v7x, 128 devices: a whole 4x4x4 slice. The times are simulated.
128 devices in a mesh: ctx: 32 (over y, z, core), tp: 4 (over x).
Axes of the slice: x: 4, y: 4, z: 4, core: 2. Of those that a mesh axis runs over, the one named last changes fastest.
Arguments:
- hidden_in: bfloat16 [16384, 4608], P('ctx'), may hold values from -5.4 to 5.4
- pre_gain: float32 [4608], replicated, may hold values from 0.25 to 1.75
- w_query: bfloat16 [4608, 2048], P(None, 'tp'), may hold values from -0.677644 to 0.677644
- w_key: bfloat16 [4608, 1024], P(None, 'tp'), may hold values from -0.058925565 to 0.058925565
- w_value: bfloat16 [4608, 1024], P(None, 'tp'), may hold values from -0.09375 to 0.09375
- w_out: bfloat16 [2048, 4608], P('tp'), may hold values from -0.26516504 to 0.26516504
- post_gain: float32 [4608], P('tp'), may hold values from 0.25 to 1.75
Outputs:
- layer_out: bfloat16 [16384, 4608], P('ctx', 'tp')
- sink_share: float32 [16384], P('ctx')
All inputs are finite; a program needn't handle non-finite values.
Results may differ from a plain program's by a relative error of at most 0.0095.
The roundings to bfloat16 on the way count: a program that leaves them out, or rounds other values in their place, can miss the bound.
Values may be sent and summed in bfloat16 or wider, within the bound.
No kernel may reach another device: no remote copies, remote signals or barrier semaphores. Data moves between devices by JAX's collectives and lax.ppermute only.
A program may use at most 192 MiB of HBM per device.

v0:
```python
import jax
import jax.numpy as jnp
from jax import lax
from jax.sharding import PartitionSpec as P

D = 4608
QHEADS = 16
HEAD = 128
WINDOW = 4096
SINKS = 4


def shifted(x, axis, by):
    devices = lax.axis_size(axis)
    pairs = [(i, i + by) for i in range(devices) if 0 <= i + by < devices]
    return lax.ppermute(x, axis, pairs)


def spread(value, axis, source):
    kept = jnp.where(lax.axis_index(axis) == source, value, 0).astype(value.dtype)
    return lax.psum(kept, axis)


def rope_tables(positions):
    index = jnp.arange(0, HEAD, 2).astype(jnp.float32)
    inverse = jnp.exp(-jnp.log(jnp.float32(10000.0)) * index / HEAD)
    angles = positions.astype(jnp.float32)[:, None] * inverse[None, :]
    angles = jnp.concatenate([angles, angles], axis=1)
    return (jnp.cos(angles)[:, None, :], jnp.sin(angles)[:, None, :])


def rotate(values, cosine_table, sine_table):
    half = values.shape[-1] // 2
    turned = jnp.concatenate([-values[..., half:], values[..., :half]], axis=-1)
    return values * cosine_table + turned * sine_table


def project_keys(states, w_key, w_value, positions):
    count = states.shape[0]
    cosine_table, sine_table = rope_tables(positions)
    keys = jnp.dot(states, w_key, preferred_element_type=jnp.float32).reshape(count, -1, HEAD)
    keys = rotate(keys, cosine_table, sine_table).astype(jnp.bfloat16).reshape(count, -1)
    values = jnp.dot(states, w_value, preferred_element_type=jnp.float32).astype(jnp.bfloat16)
    return (keys, values)


def on_device(hidden_in, pre_gain, w_query, w_key, w_value, w_out, post_gain):
    tok_rows = hidden_in.shape[0]
    local_q = w_query.shape[1] // HEAD
    local_kv = w_key.shape[1] // HEAD
    group = local_q // local_kv
    offset = lax.axis_index("ctx") * tok_rows
    inputs = hidden_in.astype(jnp.float32)
    normed = (
        inputs * lax.rsqrt(jnp.mean(inputs * inputs, axis=-1, keepdims=True) + 1e-06) * pre_gain
    ).astype(jnp.bfloat16)
    positions = offset + jnp.arange(tok_rows, dtype=jnp.int32)
    cosine_table, sine_table = rope_tables(positions)
    query = jnp.dot(normed, w_query, preferred_element_type=jnp.float32).reshape(
        tok_rows, local_q, HEAD
    )
    query = (
        rotate(query, cosine_table, sine_table)
        .astype(jnp.bfloat16)
        .reshape(tok_rows, local_kv, group, HEAD)
    )
    keys, values = project_keys(normed, w_key, w_value, positions)
    reach = WINDOW // tok_rows
    pieces = []
    for distance in range(reach, 0, -1):
        pieces.append(shifted((keys, values), "ctx", distance))
    keys_all = jnp.concatenate([piece[0] for piece in pieces] + [keys], axis=0)
    values_all = jnp.concatenate([piece[1] for piece in pieces] + [values], axis=0)
    sink_keys, sink_values = (spread(keys[:SINKS], "ctx", 0), spread(values[:SINKS], "ctx", 0))
    sink_keys = sink_keys.reshape(SINKS, local_kv, HEAD)
    sink_values = sink_values.reshape(SINKS, local_kv, HEAD)
    block_rows = min(512, tok_rows)
    span = WINDOW + block_rows

    def one_block(block_index):
        start = block_index * block_rows
        key_block = keys_all.reshape(span, local_kv, HEAD)
        value_block = values_all.reshape(span, local_kv, HEAD)
        scores = (
            jnp.einsum("qkgd,lkd->kgql", query, key_block, preferred_element_type=jnp.float32)
            / 12.0
        )
        scores = 50.0 * jnp.tanh(scores / 50.0)
        sink_scores = (
            jnp.einsum("qkgd,lkd->kgql", query, sink_keys, preferred_element_type=jnp.float32)
            / 12.0
        )
        sink_scores = 50.0 * jnp.tanh(sink_scores / 50.0)
        query_pos = offset + start + jnp.arange(block_rows, dtype=jnp.int32)
        key_pos = offset + start - WINDOW + jnp.arange(span, dtype=jnp.int32)
        distance_map = query_pos[:, None] - key_pos[None, :]
        live = (key_pos[None, :] >= SINKS) & (distance_map >= 0) & (distance_map < WINDOW)
        sink_live = query_pos[:, None] - jnp.arange(SINKS, dtype=jnp.int32)[None, :] >= 0
        expo = jnp.where(live, jnp.exp(scores), 0.0)
        sink_expo = jnp.where(sink_live, jnp.exp(sink_scores), 0.0)
        total = jnp.sum(expo, axis=-1) + jnp.sum(sink_expo, axis=-1)
        weight = expo / total[..., None]
        sink_weight = sink_expo / total[..., None]
        sink_sum = jnp.sum(sink_expo, axis=-1)
        attended = jnp.einsum(
            "kgql,lkd->qkgd",
            weight.astype(jnp.bfloat16),
            value_block,
            preferred_element_type=jnp.float32,
        )
        attended = attended + jnp.einsum(
            "kgql,lkd->qkgd",
            sink_weight.astype(jnp.bfloat16),
            sink_values,
            preferred_element_type=jnp.float32,
        )
        attended = attended.astype(jnp.bfloat16).reshape(block_rows, local_q * HEAD)
        return (attended, jnp.sum(sink_sum, axis=(0, 1)))

    attended, sink_sums = lax.map(one_block, jnp.arange(tok_rows // block_rows, dtype=jnp.int32))
    attended = attended.reshape(tok_rows, local_q * HEAD)
    sink_sums = sink_sums.reshape(tok_rows)
    cols_dev = post_gain.shape[0]
    partial_rows = jnp.dot(attended, w_out, preferred_element_type=jnp.float32)
    projected = lax.psum_scatter(partial_rows, "tp", scatter_dimension=1, tiled=True)
    squares = jnp.sum(projected * projected, axis=-1)
    total_squares, total_sinks = lax.psum((squares, sink_sums), "tp")
    post = projected * lax.rsqrt(total_squares / D + 1e-06)[:, None] * post_gain
    own_cols = lax.dynamic_slice_in_dim(inputs, lax.axis_index("tp") * cols_dev, cols_dev, 1)
    layer_out = (own_cols + post).astype(jnp.bfloat16)
    sink_share = jnp.log(total_sinks / QHEADS)
    return (layer_out, sink_share)


def solution(mesh):
    return jax.shard_map(
        on_device,
        mesh=mesh,
        in_specs=(
            P("ctx", None),
            P(),
            P(None, "tp"),
            P(None, "tp"),
            P(None, "tp"),
            P("tp", None),
            P("tp"),
        ),
        out_specs=(P("ctx", "tp"), P("ctx")),
        check_vma=False,
    )
```

profile of v0, /device:TPU:0, one launch (start us, length us, event | category | flops | bytes accessed | tf_op | source)
XLA Modules:
  0.0 350.9 jit_solution(993814466093420945)
XLA Ops:
  8.6 3.6 %multiply_reduce_fusion = f32[512]{0:T(512)S(1)} fusion(bf16[512,4608]{1,0:T(8,128)(2,1)} %param.7), kind=kLoop, calls=%fused_computation.7 | loop fusion | flops 7077376 | bytes 4720640 | tf_op jit(solution)/shard_map/reduce_sum | solution.py:55
  12.6 1.8 fusion.30
  16.2 4.4 %collective-permute-start.8 = (bf16[512,256]{0,1:T(8,128)(2,1)}, bf16[512,256]{0,1:T(8,128)(2,1)}, u32[]{:S(2)}, u32[]{:S(2)}) collective-permute-start(bf16[512,256]{0,1:T(8,128)(2,1)} %fusion.15), channel_id=1, source_target_pairs={{0,32},{4,36},{8,40},{12,44},{16,48},{20,52},{24,56},{28,60},{32,6... | collective-permute-start | bytes 786440 | tf_op jit(solution)/shard_map/ppermute | solution.py:16
  20.7 5.8 %collective-permute-start.9 = (bf16[512,256]{0,1:T(8,128)(2,1)}, bf16[512,256]{0,1:T(8,128)(2,1)}, u32[]{:S(2)}, u32[]{:S(2)}) collective-permute-start(bf16[512,256]{0,1:T(8,128)(2,1)} %fusion.15), channel_id=1, source_target_pairs={{0,28},{4,32},{8,36},{12,40},{16,44},{20,48},{24,52},{28,56},{32,6... | collective-permute-start | bytes 786440 | tf_op jit(solution)/shard_map/ppermute | solution.py:16
  26.5 3.3 collective-permute-start.10
  29.8 3.0 collective-permute-start.11
  32.8 5.2 %convolution_convert_fusion = bf16[512,256]{1,0:T(8,128)(2,1)} fusion(bf16[4608,256]{1,0:T(8,128)(2,1)} %param.11, f32[4608]{0:T(1024)S(1)} %copy-done.14, f32[512]{0:T(512)S(1)} %add_rsqrt_fusion.1, bf16[512,4608]{1,0:T(8,128)(2,1)} %param.7), kind=kOutput, calls=%fused_computation.16 | convolution fusion | flops 1217527808 | bytes 7360512 | tf_op jit(solution)/shard_map/dot_general | solution.py:43
  38.1 2.0 collective-permute-start
  40.7 6.9 %fusion.29 = f32[512,512]{0,1:T(8,128)S(1)} fusion(bf16[4608,512]{1,0:T(8,128)(2,1)} %param.9, f32[4608]{0:T(1024)S(1)} %copy-done.15, f32[512]{0:T(512)} %copy-done.13, bf16[512,4608]{1,0:T(8,128)(2,1)} %param.7), kind=kOutput, calls=%fused_computation.75 | convolution fusion | flops 2425356288 | bytes 10506240 | tf_op jit(solution)/shard_map/dot_general | solution.py:59
  53.3 4.7 %fusion.3 = pred[512,4608]{0,1:T(8,128)(4,1)} fusion(s32[4608]{0:T(1024)S(1)} %copy-done.11, s32[512]{0:T(512)S(1)} %iota_add_fusion.1, pred[4608]{0:T(1024)(128)(4,1)S(1)} %broadcast_compare_fusion), kind=kLoop, calls=%fused_computation.9 | loop fusion | flops 11796480 | bytes 2384384 | tf_op jit(solution)/shard_map/while/body/eval_jaxpr/and | solution.py:97
  59.4 62.8 %all-reduce.1 = (bf16[4,2,128]{2,0,1:T(4,128)(2,1)S(1)}, bf16[4,2,128]{2,0,1:T(4,128)(2,1)S(1)}) all-reduce(bf16[4,2,128]{2,0,1:T(4,128)(2,1)S(1)} %fusion.21, bf16[4,2,128]{2,0,1:T(4,128)(2,1)S(1)} %fusion.22), channel_id=1, replica_groups=mesh['ctx'=32,'tp'=4] {'ctx'}, use_global_device_ids=true, to_apply=%region_2.3 | all-reduce | flops 2048 | bytes 8192 | tf_op jit(solution)/shard_map/psum | solution.py:21
  133.1 7.4 %collective-permute-done.1 = bf16[512,256]{1,0:T(8,128)(2,1)S(1)} collective-permute-done((bf16[512,256]{1,0:T(8,128)(2,1)}, bf16[512,256]{1,0:T(8,128)(2,1)S(1)}, u32[]{:S(2)}, u32[]{:S(2)}) %collective-permute-start.1) | collective-permute-done | bytes 262176 | tf_op jit(solution)/shard_map/ppermute | solution.py:16
  141.9 7.1 %collective-permute-start.14 = (bf16[512,256]{0,1:T(8,128)(2,1)}, bf16[512,256]{0,1:T(8,128)(2,1)}, u32[]{:S(2)}, u32[]{:S(2)}) collective-permute-start(bf16[512,256]{0,1:T(8,128)(2,1)} %fusion.15), channel_id=1, source_target_pairs={{0,8},{4,12},{8,16},{12,20},{16,24},{20,28},{24,32},{28,36},{32,40... | collective-permute-start | bytes 786440 | tf_op jit(solution)/shard_map/ppermute | solution.py:16
  149.0 2.4 collective-permute-start.15
  151.4 2.0 collective-permute-start.5
  153.5 4.7 %collective-permute-start.6 = (bf16[512,256]{1,0:T(8,128)(2,1)}, bf16[512,256]{1,0:T(8,128)(2,1)}, u32[]{:S(2)}, u32[]{:S(2)}) collective-permute-start(bf16[512,256]{1,0:T(8,128)(2,1)} %convolution_convert_fusion), channel_id=1, source_target_pairs={{0,8},{4,12},{8,16},{12,20},{16,24},{20,28},{24,32},{28,36},{32,40... | collective-permute-start | bytes 786440 | tf_op jit(solution)/shard_map/ppermute | solution.py:16
  158.2 2.0 collective-permute-start.7
  160.2 1.8 copy.14
  162.0 1.8 copy.15
  166.2 1.8 copy.19
  168.0 1.8 copy.20
  173.8 2.5 copy.34
  176.2 1.8 constant_dynamic-update-slice_fusion.16
  183.6 1.7 constant_dynamic-update-slice_fusion.10
  186.1 17.2 %fusion = (f32[2,2,512]{2,1,0:T(2,128)S(1)}, f32[2,4608,512,2]{2,1,3,0:T(8,128)}) fusion(pred[512,4608]{0,1:T(8,128)(4,1)S(1)} %copy-done.6, bf16[512,2,2,128]{3,0,2,1:T(8,128)(2,1)S(1)} %copy-done.9, bf16[4608,2,128]{2,0,1:T(8,128)(2,1)} %constant_dynamic-update-slice_fusion.9), kind=kOutput, calls=%fused_computation.2 | convolution fusion | flops 2453665792 | bytes 42999808 | tf_op jit(solution)/shard_map/while/body/eval_jaxpr/qkgd,lkd->kgql/dot_general | solution.py:85
  203.6 19.5 %fusion.7 = bf16[2,128,2,512]{3,1,2,0:T(8,128)(2,1)} fusion(f32[2,128,2,512]{3,1,2,0:T(8,128)S(1)} %fusion.18, bf16[4608,2,128,1]{0,2,3,1:T(8,128)(2,1)} %bitcast.80, f32[2,4608,512,2]{2,1,3,0:T(8,128)} %get-tuple-element.42, f32[2,2,512]{2,1,0:T(2,128)S(1)} %add.103, pred[512,4608]{0,1:T(8,128)(4,1)S(1)} %copy-done.6), kind=kOutput, calls=%fused_computation.15 | convolution fusion | flops 2463629312 | bytes 44048384 | tf_op jit(solution)/shard_map/while/body/eval_jaxpr/kgql,lkd->qkgd/dot_general | solution.py:105
  223.1 8.8 %fusion.33 = f32[512,4608]{1,0:T(8,128)} fusion(bf16[512,512]{0,1:T(8,128)(2,1)} %bitcast.81, bf16[512,4608]{1,0:T(8,128)(2,1)} %param.12), kind=kOutput, calls=%fused_computation.79 | convolution fusion | flops 2415919104 | bytes 14680064 | tf_op jit(solution)/shard_map/dot_general | solution.py:124
  231.9 7.2 %convert_element_type.56 = f32[512,4608]{1,0:T(8,128)} convert(bf16[512,4608]{1,0:T(8,128)(2,1)} %param.7) | non-fusion elementwise | flops 2359296 | bytes 14155776 | tf_op jit(solution)/shard_map/convert_element_type | solution.py:53
  239.1 89.9 %reduce-scatter.2.cloned.1.call-done = f32[512,1152]{1,0:T(8,128)} async-done(((f32[512,4608]{1,0:T(8,128)}), f32[512,1152]{1,0:T(8,128)}) %reduce-scatter.2.cloned.1.call-update) | async-done | bytes 2359312 | tf_op jit(solution)/shard_map/reduce_scatter | solution.py:125
  329.1 1.9 multiply_reduce_fusion.1
  331.0 8.6 %all-reduce = (f32[512]{0:T(512)S(1)}, f32[512]{0:T(512)S(1)}) all-reduce(f32[512]{0:T(512)S(1)} %multiply_reduce_fusion.1, f32[512]{0:T(512)S(1)} %get-tuple-element.20), channel_id=1, replica_groups=mesh['ctx'=32,'tp'=4] {'tp'}, use_global_device_ids=true, to_apply=%region_7.8 | all-reduce | flops 1024 | bytes 8192 | tf_op jit(solution)/shard_map/psum | solution.py:127
  340.1 3.9 %add_convert_fusion = bf16[512,1152]{1,0:T(8,128)(2,1)} fusion(f32[512,1152]{1,0:T(8,128)} %reduce-scatter.2.cloned.1.call-done, f32[512,4608]{1,0:T(8,128)} %convert_element_type.56, s32[]{:T(128)S(6)} %select_n.30, f32[1152]{0:T(1024)S(1)} %copy-done.12, f32[512]{0:T(512)S(1)} %get-tuple-element.45), kind=kLoop, calls=%fused_computation.12 | loop fusion | flops 2359296 | bytes 5904900 | tf_op jit(solution)/shard_map/convert_element_type | solution.py:130
  (107 shorter events, 36.9 us)
Async XLA Ops:
  7.2 5.0 %copy-start = (bf16[4608,256]{1,0:T(8,128)(2,1)S(1)}, bf16[4608,256]{1,0:T(8,128)(2,1)}, u32[]{:S(2)}) copy-start(bf16[4608,256]{1,0:T(8,128)(2,1)} %param.10) | copy-start | bytes 7077892
  7.2 321.9 %reduce-scatter.2.cloned.1.call-start = ((), (), s32[]{:S(2)}) async-start(), calls=%async_computation.1 | async-start | bytes 11796480 | tf_op jit(solution)/shard_map/reduce_scatter | solution.py:125
  7.4 4.7 %copy-start.14 = (f32[4608]{0:T(1024)S(1)}, f32[4608]{0:T(1024)}, u32[]{:S(2)}) copy-start(f32[4608]{0:T(1024)} %param.8) | copy-start | bytes 55300
  8.5 6.3 %copy-start.5 = (f32[512,128]{1,0:T(8,128)}, f32[512,128]{1,0:T(8,128)S(1)}, u32[]{:S(2)}) copy-start(f32[512,128]{1,0:T(8,128)S(1)} %get-tuple-element.40) | copy-start | bytes 786436
  8.5 32.1 %copy-start.3 = (f32[512,128]{1,0:T(8,128)}, f32[512,128]{1,0:T(8,128)S(1)}, u32[]{:S(2)}) copy-start(f32[512,128]{1,0:T(8,128)S(1)} %get-tuple-element.39) | copy-start | bytes 786436
  8.6 4.0 %copy-start.2 = (bf16[512,4608]{1,0:T(8,128)(2,1)S(1)}, bf16[512,4608]{1,0:T(8,128)(2,1)}, u32[]{:S(2)}) copy-start(bf16[512,4608]{1,0:T(8,128)(2,1)} %param.7) | copy-start | bytes 14155780
  12.6 20.3 %copy-start.13 = (f32[512]{0:T(512)}, f32[512]{0:T(512)S(1)}, u32[]{:S(2)}) copy-start(f32[512]{0:T(512)S(1)} %add_rsqrt_fusion.1) | copy-start | bytes 6148
  15.1 23.0 %copy-start.7 = (f32[512,2,128]{2,0,1:T(8,128)}, f32[512,2,128]{2,0,1:T(8,128)S(1)}, u32[]{:S(2)}) copy-start(f32[512,2,128]{2,0,1:T(8,128)S(1)} %maximum_multiply_fusion.1) | copy-start | bytes 1572868
  16.2 24.5 %copy-start.15 = (f32[4608]{0:T(1024)S(1)}, f32[4608]{0:T(1024)}, u32[]{:S(2)}) copy-start(f32[4608]{0:T(1024)} %param.8) | copy-start | bytes 55300
  16.2 106.0 %collective-permute-start.8 = (bf16[512,256]{0,1:T(8,128)(2,1)}, bf16[512,256]{0,1:T(8,128)(2,1)}, u32[]{:S(2)}, u32[]{:S(2)}) collective-permute-start(bf16[512,256]{0,1:T(8,128)(2,1)} %fusion.15), channel_id=1, source_target_pairs={{0,32},{4,36},{8,40},{12,44},{16,48},{20,52},{24,56},{28,60},{32,6... | collective-permute-start | bytes 786440 | tf_op jit(solution)/shard_map/ppermute | solution.py:16
  20.7 105.4 %collective-permute-start.9 = (bf16[512,256]{0,1:T(8,128)(2,1)}, bf16[512,256]{0,1:T(8,128)(2,1)}, u32[]{:S(2)}, u32[]{:S(2)}) collective-permute-start(bf16[512,256]{0,1:T(8,128)(2,1)} %fusion.15), channel_id=1, source_target_pairs={{0,28},{4,32},{8,36},{12,40},{16,44},{20,48},{24,52},{28,56},{32,6... | collective-permute-start | bytes 786440 | tf_op jit(solution)/shard_map/ppermute | solution.py:16
  26.5 101.0 %collective-permute-start.10 = (bf16[512,256]{0,1:T(8,128)(2,1)}, bf16[512,256]{0,1:T(8,128)(2,1)}, u32[]{:S(2)}, u32[]{:S(2)}) collective-permute-start(bf16[512,256]{0,1:T(8,128)(2,1)} %fusion.15), channel_id=1, source_target_pairs={{0,24},{4,28},{8,32},{12,36},{16,40},{20,44},{24,48},{28,52},{32,5... | collective-permute-start | bytes 786440 | tf_op jit(solution)/shard_map/ppermute | solution.py:16
  29.8 99.0 %collective-permute-start.11 = (bf16[512,256]{0,1:T(8,128)(2,1)}, bf16[512,256]{0,1:T(8,128)(2,1)}, u32[]{:S(2)}, u32[]{:S(2)}) collective-permute-start(bf16[512,256]{0,1:T(8,128)(2,1)} %fusion.15), channel_id=1, source_target_pairs={{0,20},{4,24},{8,28},{12,32},{16,36},{20,40},{24,44},{28,48},{32,5... | collective-permute-start | bytes 786440 | tf_op jit(solution)/shard_map/ppermute | solution.py:16
  38.1 92.7 %collective-permute-start = (bf16[512,256]{1,0:T(8,128)(2,1)}, bf16[512,256]{1,0:T(8,128)(2,1)}, u32[]{:S(2)}, u32[]{:S(2)}) collective-permute-start(bf16[512,256]{1,0:T(8,128)(2,1)} %convolution_convert_fusion), channel_id=1, source_target_pairs={{0,32},{4,36},{8,40},{12,44},{16,48},{20,52},{24,56},{28,60},{32,6... | collective-permute-start | bytes 786440 | tf_op jit(solution)/shard_map/ppermute | solution.py:16
  48.6 3.1 copy-start.4
  53.3 77.5 %copy-start.8 = (bf16[512,2,2,128]{3,0,2,1:T(8,128)(2,1)}, bf16[512,2,2,128]{3,0,2,1:T(8,128)(2,1)S(1)}, u32[]{:S(2)}) copy-start(bf16[512,2,2,128]{3,0,2,1:T(8,128)(2,1)S(1)} %fusion.14) | copy-start | bytes 1572868
  122.3 18.2 %collective-permute-start.1 = (bf16[512,256]{1,0:T(8,128)(2,1)}, bf16[512,256]{1,0:T(8,128)(2,1)S(1)}, u32[]{:S(2)}, u32[]{:S(2)}) collective-permute-start(bf16[512,256]{1,0:T(8,128)(2,1)} %convolution_convert_fusion), channel_id=1, source_target_pairs={{0,28},{4,32},{8,36},{12,40},{16,44},{20,48},{24,52},{28,56},{32,6... | collective-permute-start | bytes 786440 | tf_op jit(solution)/shard_map/ppermute | solution.py:16
  126.1 15.7 %collective-permute-start.12 = (bf16[512,256]{0,1:T(8,128)(2,1)}, bf16[512,256]{0,1:T(8,128)(2,1)S(1)}, u32[]{:S(2)}, u32[]{:S(2)}) collective-permute-start(bf16[512,256]{0,1:T(8,128)(2,1)} %fusion.15), channel_id=1, source_target_pairs={{0,16},{4,20},{8,24},{12,28},{16,32},{20,36},{24,40},{28,44},{32,4... | collective-permute-start | bytes 786440 | tf_op jit(solution)/shard_map/ppermute | solution.py:16
  127.5 21.5 %collective-permute-start.13 = (bf16[512,256]{0,1:T(8,128)(2,1)}, bf16[512,256]{0,1:T(8,128)(2,1)S(1)}, u32[]{:S(2)}, u32[]{:S(2)}) collective-permute-start(bf16[512,256]{0,1:T(8,128)(2,1)} %fusion.15), channel_id=1, source_target_pairs={{0,12},{4,16},{8,20},{12,24},{16,28},{20,32},{24,36},{28,40},{32,4... | collective-permute-start | bytes 786440 | tf_op jit(solution)/shard_map/ppermute | solution.py:16
  128.8 22.7 %collective-permute-start.2 = (bf16[512,256]{1,0:T(8,128)(2,1)}, bf16[512,256]{1,0:T(8,128)(2,1)S(1)}, u32[]{:S(2)}, u32[]{:S(2)}) collective-permute-start(bf16[512,256]{1,0:T(8,128)(2,1)} %convolution_convert_fusion), channel_id=1, source_target_pairs={{0,24},{4,28},{8,32},{12,36},{16,40},{20,44},{24,48},{28,52},{32,5... | collective-permute-start | bytes 786440 | tf_op jit(solution)/shard_map/ppermute | solution.py:16
  130.8 22.6 %collective-permute-start.3 = (bf16[512,256]{1,0:T(8,128)(2,1)}, bf16[512,256]{1,0:T(8,128)(2,1)S(1)}, u32[]{:S(2)}, u32[]{:S(2)}) collective-permute-start(bf16[512,256]{1,0:T(8,128)(2,1)} %convolution_convert_fusion), channel_id=1, source_target_pairs={{0,20},{4,24},{8,28},{12,32},{16,36},{20,40},{24,44},{28,48},{32,5... | collective-permute-start | bytes 786440 | tf_op jit(solution)/shard_map/ppermute | solution.py:16
  140.5 17.6 %collective-permute-start.4 = (bf16[512,256]{1,0:T(8,128)(2,1)}, bf16[512,256]{1,0:T(8,128)(2,1)S(1)}, u32[]{:S(2)}, u32[]{:S(2)}) collective-permute-start(bf16[512,256]{1,0:T(8,128)(2,1)} %convolution_convert_fusion), channel_id=1, source_target_pairs={{0,16},{4,20},{8,24},{12,28},{16,32},{20,36},{24,40},{28,44},{32,4... | collective-permute-start | bytes 786440 | tf_op jit(solution)/shard_map/ppermute | solution.py:16
  141.9 24.4 %collective-permute-start.14 = (bf16[512,256]{0,1:T(8,128)(2,1)}, bf16[512,256]{0,1:T(8,128)(2,1)}, u32[]{:S(2)}, u32[]{:S(2)}) collective-permute-start(bf16[512,256]{0,1:T(8,128)(2,1)} %fusion.15), channel_id=1, source_target_pairs={{0,8},{4,12},{8,16},{12,20},{16,24},{20,28},{24,32},{28,36},{32,40... | collective-permute-start | bytes 786440 | tf_op jit(solution)/shard_map/ppermute | solution.py:16
  149.0 11.2 %copy-start.10 = (bf16[512,256]{0,1:T(8,128)(2,1)}, bf16[512,256]{0,1:T(8,128)(2,1)S(1)}, u32[]{:S(2)}) copy-start(bf16[512,256]{0,1:T(8,128)(2,1)S(1)} %collective-permute-done.13) | copy-start | bytes 786436
  149.0 19.0 %collective-permute-start.15 = (bf16[512,256]{0,1:T(8,128)(2,1)}, bf16[512,256]{0,1:T(8,128)(2,1)}, u32[]{:S(2)}, u32[]{:S(2)}) collective-permute-start(bf16[512,256]{0,1:T(8,128)(2,1)} %fusion.15), channel_id=1, source_target_pairs={{0,4},{4,8},{8,12},{12,16},{16,20},{20,24},{24,28},{28,32},{32,36}... | collective-permute-start | bytes 786440 | tf_op jit(solution)/shard_map/ppermute | solution.py:16
  151.4 18.4 %collective-permute-start.5 = (bf16[512,256]{1,0:T(8,128)(2,1)}, bf16[512,256]{1,0:T(8,128)(2,1)}, u32[]{:S(2)}, u32[]{:S(2)}) collective-permute-start(bf16[512,256]{1,0:T(8,128)(2,1)} %convolution_convert_fusion), channel_id=1, source_target_pairs={{0,12},{4,16},{8,20},{12,24},{16,28},{20,32},{24,36},{28,40},{32,4... | collective-permute-start | bytes 786440 | tf_op jit(solution)/shard_map/ppermute | solution.py:16
  153.5 17.3 %collective-permute-start.6 = (bf16[512,256]{1,0:T(8,128)(2,1)}, bf16[512,256]{1,0:T(8,128)(2,1)}, u32[]{:S(2)}, u32[]{:S(2)}) collective-permute-start(bf16[512,256]{1,0:T(8,128)(2,1)} %convolution_convert_fusion), channel_id=1, source_target_pairs={{0,8},{4,12},{8,16},{12,20},{16,24},{20,28},{24,32},{28,36},{32,40... | collective-permute-start | bytes 786440 | tf_op jit(solution)/shard_map/ppermute | solution.py:16
  158.2 13.6 %collective-permute-start.7 = (bf16[512,256]{1,0:T(8,128)(2,1)}, bf16[512,256]{1,0:T(8,128)(2,1)}, u32[]{:S(2)}, u32[]{:S(2)}) collective-permute-start(bf16[512,256]{1,0:T(8,128)(2,1)} %convolution_convert_fusion), channel_id=1, source_target_pairs={{0,4},{4,8},{8,12},{12,16},{16,20},{20,24},{24,28},{28,32},{32,36}... | collective-permute-start | bytes 786440 | tf_op jit(solution)/shard_map/ppermute | solution.py:16
  176.2 9.8 %copy-start.6 = (pred[512,4608]{0,1:T(8,128)(4,1)S(1)}, pred[512,4608]{0,1:T(8,128)(4,1)}, u32[]{:S(2)}) copy-start(pred[512,4608]{0,1:T(8,128)(4,1)} %fusion.3) | copy-start | bytes 7077892
  176.2 9.8 %copy-start.9 = (bf16[512,2,2,128]{3,0,2,1:T(8,128)(2,1)S(1)}, bf16[512,2,2,128]{3,0,2,1:T(8,128)(2,1)}, u32[]{:S(2)}) copy-start(bf16[512,2,2,128]{3,0,2,1:T(8,128)(2,1)} %copy-done.8) | copy-start | bytes 1572868
  239.1 101.0 %copy-start.12 = (f32[1152]{0:T(1024)S(1)}, f32[1152]{0:T(1024)}, u32[]{:S(2)}) copy-start(f32[1152]{0:T(1024)} %param.13) | copy-start | bytes 13828
  340.1 3.9 %copy-start.1 = (bf16[4608,256]{1,0:T(8,128)(2,1)S(1)}, bf16[4608,256]{1,0:T(8,128)(2,1)}, u32[]{:S(2)}) copy-start(bf16[4608,256]{1,0:T(8,128)(2,1)} %param.10) | copy-start | bytes 7077892
  (1 other events, 1.7 us)
Sparse Core Ops, SparseCore 0:
  232.0 97.0 reduce-scatter.1
where the time goes:
time: 352 us; the launch traced here: 351 us
  waiting for transfers between devices  97.4 us (28%)
  blocking collectives  71.4 us (20%)
  matrix products  60 us (17%)
  starting transfers between devices  44.7 us (13%)
  local copies, waits for them, and re-layouts  34.1 us (10%)
  other arithmetic  28.8 us (8%)
  between operations  14.5 us (4%)
    reduce_scatter x1, waiting for transfers between devices, on_device(): lax.psum_scatter(partial_rows, 'tp', scatter_dimension=1, tiled=True)  89.9 us
    psum x1, blocking collectives, spread(): return lax.psum(kept, axis)  62.8 us
    ppermute x16, starting transfers between devices, shifted(): return lax.ppermute(x, axis, pairs)  44.6 us
    dot_general x1, matrix products, one_block(): jnp.einsum('kgql,lkd->qkgd', weight.astype(jnp.bfloat16), value_block, pr...  19.5 us
    dot_general x1, matrix products, one_block(): jnp.einsum('qkgd,lkd->kgql', query, key_block, preferred_element_type=jnp...  17.2 us
    unnamed x52, local copies, waits for them, and re-layouts  14.8 us
    concatenate x10, local copies, waits for them, and re-layouts, on_device(): keys_all = jnp.concatenate([piece[0] for piece in pieces] + [keys], axis=0)  12.6 us
    dot_general x1, matrix products, on_device(): partial_rows = jnp.dot(attended, w_out, preferred_element_type=jnp.float32)  8.81 us
  transfers between devices with their start and end apart: 17, of which 2 were waited for; matrix products, arithmetic and copies ran while one was open for 14% of the time, Pallas kernels for 0%

commit v1 on v0

--- a/solution.py
+++ b/solution.py
@@ -18,7 +18,7 @@
 
 def spread(value, axis, source):
     kept = jnp.where(lax.axis_index(axis) == source, value, 0).astype(value.dtype)
-    return lax.psum(kept, axis)
+    return jnp.sum(lax.all_gather(kept, axis), axis=0)
 
 
 def rope_tables(positions):

time: 352 us -> 339 us (0.963)
  blocking collectives: 71.4 us -> 53.5 us
  starting transfers between devices: 44.7 us -> 58.5 us
  waiting for transfers between devices: 97.4 us -> 89.4 us
    psum x1 -> x0, blocking collectives: 62.8 us -> none  [spread(): return lax.psum(kept, axis)]
    all_gather x0 -> x2, blocking collectives: none -> 44.9 us  [spread(): return jnp.sum(lax.all_gather(kept, axis), axis=0)]
    ppermute x16, starting transfers between devices: 44.6 us -> 58.4 us  [shifted(): return lax.ppermute(x, axis, pairs)]
    ppermute x16, waiting for transfers between devices: 7.48 us -> 1.24 us  [shifted(): return lax.ppermute(x, axis, pairs)]
    unnamed x52 -> x48, local copies, waits for them, and re-layouts: 14.8 us -> 14.2 us
where the time goes in v1:
time: 339 us; the launch traced here: 337 us
  waiting for transfers between devices  89.4 us (26%)
  matrix products  59.2 us (17%)
  starting transfers between devices  58.5 us (17%)
  blocking collectives  53.5 us (16%)
  local copies, waits for them, and re-layouts  33.7 us (10%)
  other arithmetic  28.4 us (8%)
  between operations  14.5 us (4%)
    reduce_scatter x1, waiting for transfers between devices, on_device(): lax.psum_scatter(partial_rows, 'tp', scatter_dimension=1, tiled=True)  88.2 us
    ppermute x16, starting transfers between devices, shifted(): return lax.ppermute(x, axis, pairs)  58.4 us
    all_gather x2, blocking collectives, spread(): return jnp.sum(lax.all_gather(kept, axis), axis=0)  44.9 us
    dot_general x1, matrix products, one_block(): jnp.einsum('kgql,lkd->qkgd', weight.astype(jnp.bfloat16), value_block, pr...  19.4 us
    dot_general x1, matrix products, one_block(): jnp.einsum('qkgd,lkd->kgql', query, key_block, preferred_element_type=jnp...  17.2 us
    unnamed x48, local copies, waits for them, and re-layouts  14.2 us
    concatenate x10, local copies, waits for them, and re-layouts, on_device(): keys_all = jnp.concatenate([piece[0] for piece in pieces] + [keys], axis=0)  12.5 us
    dot_general x1, matrix products, on_device(): partial_rows = jnp.dot(attended, w_out, preferred_element_type=jnp.float32)  8.8 us
  transfers between devices with their start and end apart: 17, of which 2 were waited for; matrix products, arithmetic and copies ran while one was open for 14% of the time, Pallas kernels for 0%

profile of v1, /device:TPU:0, one launch (start us, length us, event | category | flops | bytes accessed | tf_op | source)
XLA Modules:
  0.0 337.2 jit_solution(17428150130586957969)
XLA Ops:
  8.7 3.5 %multiply_reduce_fusion = f32[512]{0:T(512)S(1)} fusion(bf16[512,4608]{1,0:T(8,128)(2,1)} %param.7), kind=kLoop, calls=%fused_computation.7 | loop fusion | flops 7077376 | bytes 4720640 | tf_op jit(solution)/shard_map/reduce_sum | solution.py:55
  15.5 4.4 %collective-permute-start.8 = (bf16[512,256]{0,1:T(8,128)(2,1)}, bf16[512,256]{0,1:T(8,128)(2,1)}, u32[]{:S(2)}, u32[]{:S(2)}) collective-permute-start(bf16[512,256]{0,1:T(8,128)(2,1)} %fusion.15), channel_id=1, source_target_pairs={{0,32},{4,36},{8,40},{12,44},{16,48},{20,52},{24,56},{28,60},{32,6... | collective-permute-start | bytes 786440 | tf_op jit(solution)/shard_map/ppermute | solution.py:16
  19.9 5.8 %collective-permute-start.9 = (bf16[512,256]{0,1:T(8,128)(2,1)}, bf16[512,256]{0,1:T(8,128)(2,1)}, u32[]{:S(2)}, u32[]{:S(2)}) collective-permute-start(bf16[512,256]{0,1:T(8,128)(2,1)} %fusion.15), channel_id=1, source_target_pairs={{0,28},{4,32},{8,36},{12,40},{16,44},{20,48},{24,52},{28,56},{32,6... | collective-permute-start | bytes 786440 | tf_op jit(solution)/shard_map/ppermute | solution.py:16
  25.7 3.3 collective-permute-start.10
  29.0 3.0 collective-permute-start.11
  32.0 4.5 %convolution_convert_fusion = bf16[512,256]{1,0:T(8,128)(2,1)} fusion(bf16[4608,256]{1,0:T(8,128)(2,1)S(1)} %copy-done.14, f32[4608]{0:T(1024)S(1)} %copy-done.15, f32[512]{0:T(512)S(1)} %add_rsqrt_fusion.1, bf16[512,4608]{1,0:T(8,128)(2,1)} %param.7), kind=kOutput, calls=%fused_computation.16 | convolution fusion | flops 1217527808 | bytes 7360512 | tf_op jit(solution)/shard_map/dot_general | solution.py:43
  36.6 2.0 collective-permute-start
  38.6 6.9 %fusion.29 = f32[512,512]{0,1:T(8,128)S(1)} fusion(bf16[4608,512]{1,0:T(8,128)(2,1)} %param.9, f32[4608]{0:T(1024)S(1)} %copy-done.15, f32[512]{0:T(512)S(1)} %add_rsqrt_fusion.1, bf16[512,4608]{1,0:T(8,128)(2,1)} %param.7), kind=kOutput, calls=%fused_computation.77 | convolution fusion | flops 2425356288 | bytes 10506240 | tf_op jit(solution)/shard_map/dot_general | solution.py:59
  52.1 4.7 %fusion.3 = pred[512,4608]{0,1:T(8,128)(4,1)} fusion(s32[4608]{0:T(1024)S(1)} %iota_add_fusion, s32[512]{0:T(512)S(1)} %get-tuple-element.42, pred[4608]{0:T(1024)(128)(4,1)S(1)} %broadcast_compare_fusion), kind=kLoop, calls=%fused_computation.9 | loop fusion | flops 11796480 | bytes 2384384 | tf_op jit(solution)/shard_map/while/body/eval_jaxpr/and | solution.py:97
  56.9 22.2 %all_gather.10 = bf16[32,4,256]{2,1,0:T(4,128)(2,1)S(1)} all-gather(bf16[1,4,256]{2,1,0:T(4,128)(2,1)S(1)} %copy.50), channel_id=1, replica_groups=mesh['ctx'=32,'tp'=4] {'ctx'}, dimensions={0}, use_global_device_ids=true | all-gather | bytes 67584 | tf_op jit(solution)/shard_map/all_gather | solution.py:21
  79.5 4.3 %collective-permute-start.1 = (bf16[512,256]{1,0:T(8,128)(2,1)}, bf16[512,256]{1,0:T(8,128)(2,1)S(1)}, u32[]{:S(2)}, u32[]{:S(2)}) collective-permute-start(bf16[512,256]{1,0:T(8,128)(2,1)} %convolution_convert_fusion), channel_id=1, source_target_pairs={{0,28},{4,32},{8,36},{12,40},{16,44},{20,48},{24,52},{28,56},{32,6... | collective-permute-start | bytes 786440 | tf_op jit(solution)/shard_map/ppermute | solution.py:16
  85.7 22.6 %all-gather.1 = bf16[32,4,256]{2,1,0:T(4,128)(2,1)S(1)} all-gather(bf16[1,4,256]{2,1,0:T(4,128)(2,1)S(1)} %fusion.22), channel_id=2, replica_groups=mesh['ctx'=32,'tp'=4] {'ctx'}, dimensions={0}, use_global_device_ids=true | all-gather | bytes 67584 | tf_op jit(solution)/shard_map/all_gather | solution.py:21
  109.5 4.0 %collective-permute-start.12 = (bf16[512,256]{0,1:T(8,128)(2,1)}, bf16[512,256]{0,1:T(8,128)(2,1)S(1)}, u32[]{:S(2)}, u32[]{:S(2)}) collective-permute-start(bf16[512,256]{0,1:T(8,128)(2,1)} %fusion.15), channel_id=1, source_target_pairs={{0,16},{4,20},{8,24},{12,28},{16,32},{20,36},{24,40},{28,44},{32,4... | collective-permute-start | bytes 786440 | tf_op jit(solution)/shard_map/ppermute | solution.py:16
  113.6 2.1 collective-permute-start.13
  115.7 4.0 %collective-permute-start.2 = (bf16[512,256]{1,0:T(8,128)(2,1)}, bf16[512,256]{1,0:T(8,128)(2,1)S(1)}, u32[]{:S(2)}, u32[]{:S(2)}) collective-permute-start(bf16[512,256]{1,0:T(8,128)(2,1)} %convolution_convert_fusion), channel_id=1, source_target_pairs={{0,24},{4,28},{8,32},{12,36},{16,40},{20,44},{24,48},{28,52},{32,5... | collective-permute-start | bytes 786440 | tf_op jit(solution)/shard_map/ppermute | solution.py:16
  120.4 3.4 %collective-permute-start.3 = (bf16[512,256]{1,0:T(8,128)(2,1)}, bf16[512,256]{1,0:T(8,128)(2,1)S(1)}, u32[]{:S(2)}, u32[]{:S(2)}) collective-permute-start(bf16[512,256]{1,0:T(8,128)(2,1)} %convolution_convert_fusion), channel_id=1, source_target_pairs={{0,20},{4,24},{8,28},{12,32},{16,36},{20,40},{24,44},{28,48},{32,5... | collective-permute-start | bytes 786440 | tf_op jit(solution)/shard_map/ppermute | solution.py:16
  124.8 4.6 %collective-permute-start.4 = (bf16[512,256]{1,0:T(8,128)(2,1)}, bf16[512,256]{1,0:T(8,128)(2,1)S(1)}, u32[]{:S(2)}, u32[]{:S(2)}) collective-permute-start(bf16[512,256]{1,0:T(8,128)(2,1)} %convolution_convert_fusion), channel_id=1, source_target_pairs={{0,16},{4,20},{8,24},{12,28},{16,32},{20,36},{24,40},{28,44},{32,4... | collective-permute-start | bytes 786440 | tf_op jit(solution)/shard_map/ppermute | solution.py:16
  129.4 4.1 %collective-permute-start.14 = (bf16[512,256]{0,1:T(8,128)(2,1)}, bf16[512,256]{0,1:T(8,128)(2,1)}, u32[]{:S(2)}, u32[]{:S(2)}) collective-permute-start(bf16[512,256]{0,1:T(8,128)(2,1)} %fusion.15), channel_id=1, source_target_pairs={{0,8},{4,12},{8,16},{12,20},{16,24},{20,28},{24,32},{28,36},{32,40... | collective-permute-start | bytes 786440 | tf_op jit(solution)/shard_map/ppermute | solution.py:16
  133.5 2.0 collective-permute-start.15
  136.7 2.0 collective-permute-start.5
  138.7 5.1 %collective-permute-start.6 = (bf16[512,256]{1,0:T(8,128)(2,1)}, bf16[512,256]{1,0:T(8,128)(2,1)}, u32[]{:S(2)}, u32[]{:S(2)}) collective-permute-start(bf16[512,256]{1,0:T(8,128)(2,1)} %convolution_convert_fusion), channel_id=1, source_target_pairs={{0,8},{4,12},{8,16},{12,20},{16,24},{20,28},{24,32},{28,36},{32,40... | collective-permute-start | bytes 786440 | tf_op jit(solution)/shard_map/ppermute | solution.py:16
  143.8 4.3 %collective-permute-start.7 = (bf16[512,256]{1,0:T(8,128)(2,1)}, bf16[512,256]{1,0:T(8,128)(2,1)}, u32[]{:S(2)}, u32[]{:S(2)}) collective-permute-start(bf16[512,256]{1,0:T(8,128)(2,1)} %convolution_convert_fusion), channel_id=1, source_target_pairs={{0,4},{4,8},{8,12},{12,16},{16,20},{20,24},{24,28},{28,32},{32,36}... | collective-permute-start | bytes 786440 | tf_op jit(solution)/shard_map/ppermute | solution.py:16
  161.7 2.6 copy.49
  164.3 1.9 constant_dynamic-update-slice_fusion.16
  174.2 17.2 %fusion = (f32[2,2,512]{2,1,0:T(2,128)S(1)}, f32[2,4608,512,2]{2,1,3,0:T(8,128)}) fusion(pred[512,4608]{0,1:T(8,128)(4,1)S(1)} %copy-done.8, bf16[512,2,2,128]{3,0,2,1:T(8,128)(2,1)S(1)} %copy-done.10, bf16[4608,2,128]{2,0,1:T(8,128)(2,1)} %constant_dynamic-update-slice_fusion.9), kind=kOutput, calls=%fused_computation.2 | convolution fusion | flops 2453665792 | bytes 42999808 | tf_op jit(solution)/shard_map/while/body/eval_jaxpr/qkgd,lkd->kgql/dot_general | solution.py:85
  191.7 19.4 %fusion.7 = bf16[2,128,2,512]{3,1,2,0:T(8,128)(2,1)} fusion(f32[2,128,2,512]{3,1,2,0:T(8,128)S(1)} %fusion.20, bf16[4608,2,128,1]{0,2,3,1:T(8,128)(2,1)} %bitcast.86, f32[2,4608,512,2]{2,1,3,0:T(8,128)} %get-tuple-element.40, f32[2,2,512]{2,1,0:T(2,128)S(1)} %add.99, pred[512,4608]{0,1:T(8,128)(4,1)S(1)} %copy-done.8), kind=kOutput, calls=%fused_computation.15 | convolution fusion | flops 2463629312 | bytes 44048384 | tf_op jit(solution)/shard_map/while/body/eval_jaxpr/kgql,lkd->qkgd/dot_general | solution.py:105
  211.2 8.8 %fusion.32 = f32[512,4608]{1,0:T(8,128)} fusion(bf16[512,512]{0,1:T(8,128)(2,1)} %bitcast.87, bf16[512,4608]{1,0:T(8,128)(2,1)} %param.12), kind=kOutput, calls=%fused_computation.80 | convolution fusion | flops 2415919104 | bytes 14680064 | tf_op jit(solution)/shard_map/dot_general | solution.py:124
  220.0 7.2 %convert_element_type.60 = f32[512,4608]{1,0:T(8,128)} convert(bf16[512,4608]{1,0:T(8,128)(2,1)} %param.7) | non-fusion elementwise | flops 2359296 | bytes 14155776 | tf_op jit(solution)/shard_map/convert_element_type | solution.py:53
  227.2 88.2 %reduce-scatter.2.cloned.1.call-done = f32[512,1152]{1,0:T(8,128)} async-done(((f32[512,4608]{1,0:T(8,128)}), f32[512,1152]{1,0:T(8,128)}) %reduce-scatter.2.cloned.1.call-update) | async-done | bytes 2359312 | tf_op jit(solution)/shard_map/reduce_scatter | solution.py:125
  315.4 1.9 multiply_reduce_fusion.1
  317.3 8.6 %all-reduce = (f32[512]{0:T(512)S(1)}, f32[512]{0:T(512)S(1)}) all-reduce(f32[512]{0:T(512)S(1)} %multiply_reduce_fusion.1, f32[512]{0:T(512)S(1)} %get-tuple-element.20), channel_id=1, replica_groups=mesh['ctx'=32,'tp'=4] {'tp'}, use_global_device_ids=true, to_apply=%region_7.8 | all-reduce | flops 1024 | bytes 8192 | tf_op jit(solution)/shard_map/psum | solution.py:127
  326.5 3.8 %add_convert_fusion = bf16[512,1152]{1,0:T(8,128)(2,1)} fusion(f32[512,1152]{1,0:T(8,128)} %reduce-scatter.2.cloned.1.call-done, f32[512,4608]{1,0:T(8,128)} %convert_element_type.60, s32[]{:T(128)S(6)} %select_n.37, f32[1152]{0:T(1024)S(1)} %copy-done.13, f32[512]{0:T(512)S(1)} %add_rsqrt_fusion), kind=kLoop, calls=%fused_computation.12 | loop fusion | flops 2359296 | bytes 5904900 | tf_op jit(solution)/shard_map/convert_element_type | solution.py:130
  (107 shorter events, 40.1 us)
Async XLA Ops:
  7.2 5.0 %copy-start = (bf16[4608,256]{1,0:T(8,128)(2,1)S(1)}, bf16[4608,256]{1,0:T(8,128)(2,1)}, u32[]{:S(2)}) copy-start(bf16[4608,256]{1,0:T(8,128)(2,1)} %param.10) | copy-start | bytes 7077892
  7.2 308.2 %reduce-scatter.2.cloned.1.call-start = ((), (), s32[]{:S(2)}) async-start(), calls=%async_computation.1 | async-start | bytes 11796480 | tf_op jit(solution)/shard_map/reduce_scatter | solution.py:125
  8.5 5.8 %copy-start.5 = (f32[512,128]{1,0:T(8,128)}, f32[512,128]{1,0:T(8,128)S(1)}, u32[]{:S(2)}) copy-start(f32[512,128]{1,0:T(8,128)S(1)} %get-tuple-element.37) | copy-start | bytes 786436
  8.5 3.7 %copy-start.15 = (f32[4608]{0:T(1024)S(1)}, f32[4608]{0:T(1024)}, u32[]{:S(2)}) copy-start(f32[4608]{0:T(1024)} %param.8) | copy-start | bytes 55300
  8.7 3.8 %copy-start.2 = (bf16[512,4608]{1,0:T(8,128)(2,1)S(1)}, bf16[512,4608]{1,0:T(8,128)(2,1)}, u32[]{:S(2)}) copy-start(bf16[512,4608]{1,0:T(8,128)(2,1)} %param.7) | copy-start | bytes 14155780
  14.3 22.3 %copy-start.3 = (f32[512,256]{0,1:T(8,128)}, f32[512,256]{0,1:T(8,128)S(1)}, u32[]{:S(2)}) copy-start(f32[512,256]{0,1:T(8,128)S(1)} %fusion.30) | copy-start | bytes 1572868
  14.5 24.1 %copy-start.11 = (f32[512,128]{0,1:T(8,128)}, f32[512,128]{0,1:T(8,128)S(1)}, u32[]{:S(2)}) copy-start(f32[512,128]{0,1:T(8,128)S(1)} %copy.25) | copy-start | bytes 786436
  14.5 17.5 %copy-start.14 = (bf16[4608,256]{1,0:T(8,128)(2,1)S(1)}, bf16[4608,256]{1,0:T(8,128)(2,1)}, u32[]{:S(2)}) copy-start(bf16[4608,256]{1,0:T(8,128)(2,1)} %param.11) | copy-start | bytes 7077892
  14.6 22.0 %copy-start.4 = (f32[512,2,128]{0,2,1:T(8,128)}, f32[512,2,128]{0,2,1:T(8,128)S(1)}, u32[]{:S(2)}) copy-start(f32[512,2,128]{0,2,1:T(8,128)S(1)} %maximum_multiply_fusion.1) | copy-start | bytes 1572868
  15.5 64.0 %collective-permute-start.8 = (bf16[512,256]{0,1:T(8,128)(2,1)}, bf16[512,256]{0,1:T(8,128)(2,1)}, u32[]{:S(2)}, u32[]{:S(2)}) collective-permute-start(bf16[512,256]{0,1:T(8,128)(2,1)} %fusion.15), channel_id=1, source_target_pairs={{0,32},{4,36},{8,40},{12,44},{16,48},{20,52},{24,56},{28,60},{32,6... | collective-permute-start | bytes 786440 | tf_op jit(solution)/shard_map/ppermute | solution.py:16
  19.9 89.6 %collective-permute-start.9 = (bf16[512,256]{0,1:T(8,128)(2,1)}, bf16[512,256]{0,1:T(8,128)(2,1)}, u32[]{:S(2)}, u32[]{:S(2)}) collective-permute-start(bf16[512,256]{0,1:T(8,128)(2,1)} %fusion.15), channel_id=1, source_target_pairs={{0,28},{4,32},{8,36},{12,40},{16,44},{20,48},{24,52},{28,56},{32,6... | collective-permute-start | bytes 786440 | tf_op jit(solution)/shard_map/ppermute | solution.py:16
  25.7 87.9 %collective-permute-start.10 = (bf16[512,256]{0,1:T(8,128)(2,1)}, bf16[512,256]{0,1:T(8,128)(2,1)}, u32[]{:S(2)}, u32[]{:S(2)}) collective-permute-start(bf16[512,256]{0,1:T(8,128)(2,1)} %fusion.15), channel_id=1, source_target_pairs={{0,24},{4,28},{8,32},{12,36},{16,40},{20,44},{24,48},{28,52},{32,5... | collective-permute-start | bytes 786440 | tf_op jit(solution)/shard_map/ppermute | solution.py:16
  29.0 86.7 %collective-permute-start.11 = (bf16[512,256]{0,1:T(8,128)(2,1)}, bf16[512,256]{0,1:T(8,128)(2,1)}, u32[]{:S(2)}, u32[]{:S(2)}) collective-permute-start(bf16[512,256]{0,1:T(8,128)(2,1)} %fusion.15), channel_id=1, source_target_pairs={{0,20},{4,24},{8,28},{12,32},{16,36},{20,40},{24,44},{28,48},{32,5... | collective-permute-start | bytes 786440 | tf_op jit(solution)/shard_map/ppermute | solution.py:16
  36.6 83.8 %collective-permute-start = (bf16[512,256]{1,0:T(8,128)(2,1)}, bf16[512,256]{1,0:T(8,128)(2,1)}, u32[]{:S(2)}, u32[]{:S(2)}) collective-permute-start(bf16[512,256]{1,0:T(8,128)(2,1)} %convolution_convert_fusion), channel_id=1, source_target_pairs={{0,32},{4,36},{8,40},{12,44},{16,48},{20,52},{24,56},{28,60},{32,6... | collective-permute-start | bytes 786440 | tf_op jit(solution)/shard_map/ppermute | solution.py:16
  46.7 3.7 %copy-start.6 = (f32[512,128]{1,0:T(8,128)S(1)}, f32[512,128]{1,0:T(8,128)}, u32[]{:S(2)}) copy-start(f32[512,128]{1,0:T(8,128)} %copy-done.5) | copy-start | bytes 786436
  52.1 68.3 %copy-start.9 = (bf16[512,2,2,128]{3,0,2,1:T(8,128)(2,1)}, bf16[512,2,2,128]{3,0,2,1:T(8,128)(2,1)S(1)}, u32[]{:S(2)}) copy-start(bf16[512,2,2,128]{3,0,2,1:T(8,128)(2,1)S(1)} %fusion.14) | copy-start | bytes 1572868
  79.5 45.3 %collective-permute-start.1 = (bf16[512,256]{1,0:T(8,128)(2,1)}, bf16[512,256]{1,0:T(8,128)(2,1)S(1)}, u32[]{:S(2)}, u32[]{:S(2)}) collective-permute-start(bf16[512,256]{1,0:T(8,128)(2,1)} %convolution_convert_fusion), channel_id=1, source_target_pairs={{0,28},{4,32},{8,36},{12,40},{16,44},{20,48},{24,52},{28,56},{32,6... | collective-permute-start | bytes 786440 | tf_op jit(solution)/shard_map/ppermute | solution.py:16
  109.5 19.9 %collective-permute-start.12 = (bf16[512,256]{0,1:T(8,128)(2,1)}, bf16[512,256]{0,1:T(8,128)(2,1)S(1)}, u32[]{:S(2)}, u32[]{:S(2)}) collective-permute-start(bf16[512,256]{0,1:T(8,128)(2,1)} %fusion.15), channel_id=1, source_target_pairs={{0,16},{4,20},{8,24},{12,28},{16,32},{20,36},{24,40},{28,44},{32,4... | collective-permute-start | bytes 786440 | tf_op jit(solution)/shard_map/ppermute | solution.py:16
  113.6 19.9 %collective-permute-start.13 = (bf16[512,256]{0,1:T(8,128)(2,1)}, bf16[512,256]{0,1:T(8,128)(2,1)S(1)}, u32[]{:S(2)}, u32[]{:S(2)}) collective-permute-start(bf16[512,256]{0,1:T(8,128)(2,1)} %fusion.15), channel_id=1, source_target_pairs={{0,12},{4,16},{8,20},{12,24},{16,28},{20,32},{24,36},{28,40},{32,4... | collective-permute-start | bytes 786440 | tf_op jit(solution)/shard_map/ppermute | solution.py:16
  115.7 21.0 %collective-permute-start.2 = (bf16[512,256]{1,0:T(8,128)(2,1)}, bf16[512,256]{1,0:T(8,128)(2,1)S(1)}, u32[]{:S(2)}, u32[]{:S(2)}) collective-permute-start(bf16[512,256]{1,0:T(8,128)(2,1)} %convolution_convert_fusion), channel_id=1, source_target_pairs={{0,24},{4,28},{8,32},{12,36},{16,40},{20,44},{24,48},{28,52},{32,5... | collective-permute-start | bytes 786440 | tf_op jit(solution)/shard_map/ppermute | solution.py:16
  120.4 18.3 %collective-permute-start.3 = (bf16[512,256]{1,0:T(8,128)(2,1)}, bf16[512,256]{1,0:T(8,128)(2,1)S(1)}, u32[]{:S(2)}, u32[]{:S(2)}) collective-permute-start(bf16[512,256]{1,0:T(8,128)(2,1)} %convolution_convert_fusion), channel_id=1, source_target_pairs={{0,20},{4,24},{8,28},{12,32},{16,36},{20,40},{24,44},{28,48},{32,5... | collective-permute-start | bytes 786440 | tf_op jit(solution)/shard_map/ppermute | solution.py:16
  124.8 19.0 %collective-permute-start.4 = (bf16[512,256]{1,0:T(8,128)(2,1)}, bf16[512,256]{1,0:T(8,128)(2,1)S(1)}, u32[]{:S(2)}, u32[]{:S(2)}) collective-permute-start(bf16[512,256]{1,0:T(8,128)(2,1)} %convolution_convert_fusion), channel_id=1, source_target_pairs={{0,16},{4,20},{8,24},{12,28},{16,32},{20,36},{24,40},{28,44},{32,4... | collective-permute-start | bytes 786440 | tf_op jit(solution)/shard_map/ppermute | solution.py:16
  129.4 24.8 %collective-permute-start.14 = (bf16[512,256]{0,1:T(8,128)(2,1)}, bf16[512,256]{0,1:T(8,128)(2,1)}, u32[]{:S(2)}, u32[]{:S(2)}) collective-permute-start(bf16[512,256]{0,1:T(8,128)(2,1)} %fusion.15), channel_id=1, source_target_pairs={{0,8},{4,12},{8,16},{12,20},{16,24},{20,28},{24,32},{28,36},{32,40... | collective-permute-start | bytes 786440 | tf_op jit(solution)/shard_map/ppermute | solution.py:16
  133.5 14.7 %copy-start.12 = (bf16[512,256]{0,1:T(8,128)(2,1)}, bf16[512,256]{0,1:T(8,128)(2,1)S(1)}, u32[]{:S(2)}) copy-start(bf16[512,256]{0,1:T(8,128)(2,1)S(1)} %collective-permute-done.13) | copy-start | bytes 786436
  133.5 22.5 %collective-permute-start.15 = (bf16[512,256]{0,1:T(8,128)(2,1)}, bf16[512,256]{0,1:T(8,128)(2,1)}, u32[]{:S(2)}, u32[]{:S(2)}) collective-permute-start(bf16[512,256]{0,1:T(8,128)(2,1)} %fusion.15), channel_id=1, source_target_pairs={{0,4},{4,8},{8,12},{12,16},{16,20},{20,24},{24,28},{28,32},{32,36}... | collective-permute-start | bytes 786440 | tf_op jit(solution)/shard_map/ppermute | solution.py:16
  136.7 21.1 %collective-permute-start.5 = (bf16[512,256]{1,0:T(8,128)(2,1)}, bf16[512,256]{1,0:T(8,128)(2,1)}, u32[]{:S(2)}, u32[]{:S(2)}) collective-permute-start(bf16[512,256]{1,0:T(8,128)(2,1)} %convolution_convert_fusion), channel_id=1, source_target_pairs={{0,12},{4,16},{8,20},{12,24},{16,28},{20,32},{24,36},{28,40},{32,4... | collective-permute-start | bytes 786440 | tf_op jit(solution)/shard_map/ppermute | solution.py:16
  138.7 20.1 %collective-permute-start.6 = (bf16[512,256]{1,0:T(8,128)(2,1)}, bf16[512,256]{1,0:T(8,128)(2,1)}, u32[]{:S(2)}, u32[]{:S(2)}) collective-permute-start(bf16[512,256]{1,0:T(8,128)(2,1)} %convolution_convert_fusion), channel_id=1, source_target_pairs={{0,8},{4,12},{8,16},{12,20},{16,24},{20,28},{24,32},{28,36},{32,40... | collective-permute-start | bytes 786440 | tf_op jit(solution)/shard_map/ppermute | solution.py:16
  143.8 15.9 %collective-permute-start.7 = (bf16[512,256]{1,0:T(8,128)(2,1)}, bf16[512,256]{1,0:T(8,128)(2,1)}, u32[]{:S(2)}, u32[]{:S(2)}) collective-permute-start(bf16[512,256]{1,0:T(8,128)(2,1)} %convolution_convert_fusion), channel_id=1, source_target_pairs={{0,4},{4,8},{8,12},{12,16},{16,20},{20,24},{24,28},{28,32},{32,36}... | collective-permute-start | bytes 786440 | tf_op jit(solution)/shard_map/ppermute | solution.py:16
  164.3 9.9 %copy-start.8 = (pred[512,4608]{0,1:T(8,128)(4,1)S(1)}, pred[512,4608]{0,1:T(8,128)(4,1)}, u32[]{:S(2)}) copy-start(pred[512,4608]{0,1:T(8,128)(4,1)} %fusion.3) | copy-start | bytes 7077892
  164.3 9.9 %copy-start.10 = (bf16[512,2,2,128]{3,0,2,1:T(8,128)(2,1)S(1)}, bf16[512,2,2,128]{3,0,2,1:T(8,128)(2,1)}, u32[]{:S(2)}) copy-start(bf16[512,2,2,128]{3,0,2,1:T(8,128)(2,1)} %copy-done.9) | copy-start | bytes 1572868
  227.2 99.3 %copy-start.13 = (f32[1152]{0:T(1024)S(1)}, f32[1152]{0:T(1024)}, u32[]{:S(2)}) copy-start(f32[1152]{0:T(1024)} %param.13) | copy-start | bytes 13828
  325.9 4.4 %copy-start.1 = (bf16[4608,256]{1,0:T(8,128)(2,1)S(1)}, bf16[4608,256]{1,0:T(8,128)(2,1)}, u32[]{:S(2)}) copy-start(bf16[4608,256]{1,0:T(8,128)(2,1)} %param.10) | copy-start | bytes 7077892
  (2 other events, 6.8 us)
Sparse Core Ops, SparseCore 0:
  220.1 95.2 reduce-scatter.1
